TPU v7x, 128 devices: a whole 4x4x4 slice. The times are simulated.
128 devices in a mesh: row: 8 (over z, core), col: 8 (over y_lo, x), dep: 2 (over y_hi).
Axes of the slice: x: 4, y: 4 (y_hi: 2, y_lo: 2; y = y_hi * 2 + y_lo), z: 4, core: 2. Of those that a mesh axis runs over, the one named last changes fastest.
Arguments:
- tokens: bfloat16 [2048, 8192], P(('dep', 'col'), 'row'), may hold values from -6 to 6
- gate_weight: bfloat16 [8192, 14336], P('row', 'col'), may hold values from -0.0625 to 0.0625
- up_weight: bfloat16 [8192, 14336], P('row', 'col'), may hold values from -0.0625 to 0.0625
- cotangent: bfloat16 [2048, 14336], P(('dep', 'row'), 'col'), may hold values from -6 to 6
Outputs:
- hidden: bfloat16 [2048, 14336], P(('dep', 'row'), 'col')
- grad_tokens: bfloat16 [2048, 8192], P(('dep', 'col'), 'row')
- grad_gate_weight: bfloat16 [8192, 14336], P('row', ('col', 'dep'))
- grad_up_weight: bfloat16 [8192, 14336], P('row', ('col', 'dep'))
All inputs are finite; a program needn't handle non-finite values.
Results may differ from a plain program's by a relative error of at most 0.02.
Values may be sent and summed in bfloat16 or wider, within the bound.
No kernel may reach another device: no remote copies, remote signals or barrier semaphores. Data moves between devices by JAX's collectives and lax.ppermute only.
A program may use at most 128 MiB of HBM per device.

v0:
```python
import jax
import jax.numpy as jnp
from jax import lax
from jax.sharding import PartitionSpec as P


def halves(x, dep, half):
    own = lax.dynamic_slice_in_dim(x, dep * half, half, axis=1)
    other = lax.dynamic_slice_in_dim(x, (1 - dep) * half, half, axis=1)
    return (own, other)


def on_device(tokens, gate_weight, up_weight, cotangent):
    width = gate_weight.shape[1]
    half = width // 2
    dep = lax.axis_index("dep")
    n_col = lax.axis_size("col")
    contract = (((0,), (0,)), ((), ()))
    transposed = (((1,), (1,)), ((), ()))
    pair = [(0, 1), (1, 0)]

    def gather_col(block):
        return lax.all_to_all(jnp.tile(block, (n_col, 1)), "col", 0, 0, tiled=True)

    partner_tokens = lax.ppermute(tokens, "dep", pair)
    gathered = gather_col(tokens)
    first = jnp.dot(gathered, gate_weight, preferred_element_type=jnp.float32)
    second = jnp.dot(gathered, up_weight, preferred_element_type=jnp.float32)
    joined = lax.psum_scatter(
        jnp.concatenate([first, second], axis=1).astype(jnp.bfloat16),
        "row",
        scatter_dimension=0,
        tiled=True,
    )
    gathered_partner = gather_col(partner_tokens)
    joined, gathered_partner = lax.optimization_barrier((joined, gathered_partner))
    gate = joined[:, :width]
    up = joined[:, width:]
    upstream = cotangent

    def grads(gate, up, upstream):
        gate, up, upstream = (x.astype(jnp.float32) for x in (gate, up, upstream))
        sigma = jax.nn.sigmoid(gate)
        active = gate * sigma
        grad_gate = (upstream * up * sigma * (1.0 + gate * (1.0 - sigma))).astype(jnp.bfloat16)
        return (grad_gate, (upstream * active).astype(jnp.bfloat16))

    gate_own, gate_other = halves(gate, dep, half)
    up_own, up_other = halves(up, dep, half)
    up_stream_own, up_stream_other = halves(upstream, dep, half)
    grad_gate_other, grad_up_other = grads(gate_other, up_other, up_stream_other)
    payload = jnp.concatenate([grad_gate_other, grad_up_other], axis=1)
    payload, gate_own, up_own, up_stream_own, gate, up = lax.optimization_barrier(
        (payload, gate_own, up_own, up_stream_own, gate, up)
    )
    partner_gate, partner_up = jnp.split(lax.ppermute(payload, "dep", pair), 2, axis=1)
    grad_gate_own, grad_up_own = grads(gate_own, up_own, up_stream_own)
    gate, up = (gate.astype(jnp.float32), up.astype(jnp.float32))
    hidden = (gate * jax.nn.sigmoid(gate) * up).astype(jnp.bfloat16)
    gate_own, up_own, gate_other, up_other = (
        grad_gate_own,
        grad_up_own,
        grad_gate_other,
        grad_up_other,
    )
    full = lax.all_gather(
        jnp.concatenate([gate_own, up_own, gate_other, up_other, partner_gate, partner_up], axis=1),
        "row",
        axis=0,
        tiled=True,
    )
    wg_own, wg_other = halves(gate_weight, dep, half)
    wu_own, wu_other = halves(up_weight, dep, half)
    weights = jnp.concatenate([wg_own, wu_own, wg_other, wu_other], axis=1)
    term = lax.dot_general(
        full[:, : 2 * width], weights, transposed, preferred_element_type=jnp.float32
    )
    term = term.astype(jnp.bfloat16).reshape(n_col, -1, term.shape[1])
    term, gathered, gathered_partner = lax.optimization_barrier((term, gathered, gathered_partner))
    parts = lax.all_to_all(term, "col", 0, 0, tiled=True)
    grad_tokens = parts.astype(jnp.float32).sum(axis=0).astype(jnp.bfloat16)

    def weight_grad(own, partner):
        mine = lax.dot_general(gathered, own, contract, preferred_element_type=jnp.float32)
        theirs = lax.dot_general(
            gathered_partner, partner, contract, preferred_element_type=jnp.float32
        )
        return (
            mine.astype(jnp.bfloat16).astype(jnp.float32)
            + theirs.astype(jnp.bfloat16).astype(jnp.float32)
        ).astype(jnp.bfloat16)

    sum_gate = weight_grad(full[:, :half], full[:, 2 * width : 2 * width + half])
    sum_up = weight_grad(full[:, half:width], full[:, 2 * width + half :])
    return (hidden, grad_tokens, sum_gate, sum_up)


def solution(mesh):
    return jax.shard_map(
        on_device,
        mesh=mesh,
        in_specs=(
            P(("dep", "col"), "row"),
            P("row", "col"),
            P("row", "col"),
            P(("dep", "row"), "col"),
        ),
        out_specs=(
            P(("dep", "row"), "col"),
            P(("dep", "col"), "row"),
            P("row", ("col", "dep")),
            P("row", ("col", "dep")),
        ),
        check_vma=False,
    )
```

profile of v0, /device:TPU:6, one launch (start us, length us, event | category | flops | bytes accessed | tf_op | source)
XLA Modules:
  0.0 237.5 jit_solution(15468545211119573866)
XLA Ops:
  7.2 1.2 tile.4
  8.4 30.9 %all_to_all.23 = bf16[8,128,1024]{2,1,0:T(8,128)(2,1)S(1)} all-to-all(bf16[8,128,1024]{2,1,0:T(8,128)(2,1)S(1)} %tile.4), channel_id=1, replica_groups=mesh['row'=8,'col'=8,'dep'=2] {'col'}, dimensions={0} | all-to-all | bytes 4194304 | tf_op jit(solution)/shard_map/all_to_all | solution.py:23
  39.4 4.2 %convolution_convert_fusion = bf16[1024,1792]{1,0:T(8,128)(2,1)S(1)} fusion(bf16[1024,1024]{1,0:T(8,128)(2,1)S(1)} %bitcast.11, bf16[1024,1792]{1,0:T(8,128)(2,1)S(1)} %copy-done), kind=kOutput, calls=%fused_computation.10 | convolution fusion | flops 3759931392 | bytes 9437184 | tf_op jit(solution)/shard_map/dot_general | solution.py:28
  43.5 5.4 %convolution_convert_fusion.1 = bf16[1024,1792]{1,0:T(8,128)(2,1)} fusion(bf16[1024,1024]{1,0:T(8,128)(2,1)S(1)} %bitcast.12, bf16[1024,1792]{1,0:T(8,128)(2,1)S(1)} %copy-done.1), kind=kOutput, calls=%fused_computation.11 | convolution fusion | flops 3759931392 | bytes 9437184 | tf_op jit(solution)/shard_map/dot_general | solution.py:27
  48.9 5.5 %pad_maximum_fusion = bf16[1024,3584]{1,0:T(8,128)(2,1)} fusion(bf16[1024,1792]{1,0:T(8,128)(2,1)S(1)} %convolution_convert_fusion, bf16[1024,1792]{1,0:T(8,128)(2,1)} %convolution_convert_fusion.1), kind=kLoop, calls=%fused_computation.2 | loop fusion | flops 14680064 | bytes 14680064 | tf_op jit(solution)/shard_map/concatenate | solution.py:30
  55.4 2.9 %collective-permute-start = (bf16[128,1024]{1,0:T(8,128)(2,1)S(1)}, bf16[128,1024]{1,0:T(8,128)(2,1)S(1)}, u32[]{:S(2)}, u32[]{:S(2)}) collective-permute-start(bf16[128,1024]{1,0:T(8,128)(2,1)S(1)} %copy-done.7), channel_id=1, source_target_pairs={{0,1},{1,0},{2,3},{3,2},{4,5},{5,4},{6,7},{7,6},{8,9},{9,8},{10,11... | collective-permute-start | bytes 786440 | tf_op jit(solution)/shard_map/ppermute | solution.py:25
  58.3 5.2 %collective-permute-done = bf16[128,1024]{1,0:T(8,128)(2,1)S(1)} collective-permute-done((bf16[128,1024]{1,0:T(8,128)(2,1)S(1)}, bf16[128,1024]{1,0:T(8,128)(2,1)S(1)}, u32[]{:S(2)}, u32[]{:S(2)}) %collective-permute-start) | collective-permute-done | bytes 262176 | tf_op jit(solution)/shard_map/ppermute | solution.py:25
  63.5 1.6 tile.5
  65.1 5.9 %all-to-all-start.1 = ((bf16[8,128,1024]{2,1,0:T(8,128)(2,1)}), bf16[8,128,1024]{2,1,0:T(8,128)(2,1)S(1)}, u32[]{:S(2)}, u32[]{:S(2)}) async-start(bf16[8,128,1024]{2,1,0:T(8,128)(2,1)} %tile.5), calls=%async_computation.2 | async-start | bytes 4194304 | tf_op jit(solution)/shard_map/all_to_all | solution.py:23
  71.1 22.6 %all-to-all-done.1 = bf16[8,128,1024]{2,1,0:T(8,128)(2,1)S(1)} async-done(((bf16[8,128,1024]{2,1,0:T(8,128)(2,1)}), bf16[8,128,1024]{2,1,0:T(8,128)(2,1)S(1)}, u32[]{:S(2)}, u32[]{:S(2)}) %all-to-all-start.1) | async-done | bytes 2097184 | tf_op jit(solution)/shard_map/all_to_all | solution.py:23
  93.7 10.4 %reduce-scatter.2.cloned.1.call-done = bf16[128,3584]{1,0:T(8,128)(2,1)} async-done(((bf16[1024,3584]{1,0:T(8,128)(2,1)}), bf16[128,3584]{1,0:T(8,128)(2,1)}) %reduce-scatter.2.cloned.1.call-update) | async-done | bytes 917520 | tf_op jit(solution)/shard_map/reduce_scatter | solution.py:29
  104.1 1.2 fusion.50
  105.7 3.1 %collective-permute-start.1 = (bf16[128,1792]{1,0:T(8,128)(2,1)S(1)}, bf16[128,1792]{1,0:T(8,128)(2,1)S(1)}, u32[]{:S(2)}, u32[]{:S(2)}) collective-permute-start(bf16[128,1792]{1,0:T(8,128)(2,1)S(1)} %pad_maximum_fusion.1), channel_id=1, source_target_pairs={{0,1},{1,0},{2,3},{3,2},{4,5},{5,4},{6,7},{7,6},{8,9},{9,8},{10,11... | collective-permute-start | bytes 1376264 | tf_op jit(solution)/shard_map/ppermute | solution.py:56
  112.0 6.8 %collective-permute-done.1 = bf16[128,1792]{1,0:T(8,128)(2,1)S(1)} collective-permute-done((bf16[128,1792]{1,0:T(8,128)(2,1)S(1)}, bf16[128,1792]{1,0:T(8,128)(2,1)S(1)}, u32[]{:S(2)}, u32[]{:S(2)}) %collective-permute-start.1) | collective-permute-done | bytes 458784 | tf_op jit(solution)/shard_map/ppermute | solution.py:56
  119.7 5.8 %constant_dynamic-slice_fusion.1 = (bf16[1024,896]{1,0:T(8,128)(2,1)S(1)}, bf16[1024,896]{1,0:T(8,128)(2,1)}, bf16[1024,896]{1,0:T(8,128)(2,1)}, bf16[1024,896]{1,0:T(8,128)(2,1)}) fusion(bf16[1024,1792]{1,0:T(8,128)(2,1)} %param.6, s32[]{:T(128)S(6)} %select_n.5, s32[]{:T(128)S(6)} %select_n.4, bf16[1024,1792]{1,0:T(8,128)(2,1)} %param.5), kind=kLoop, calls=%fused_computation.63 | loop fusion | bytes 14680072 | tf_op jit(solution)/shard_map/dynamic_slice | solution.py:8
  126.6 54.8 %all-gather.2.cloned.1.call-done = bf16[1024,5376]{1,0:T(8,128)(2,1)} async-done(((bf16[128,5376]{1,0:T(8,128)(2,1)}), bf16[1024,5376]{1,0:T(8,128)(2,1)}) %all-gather.2.cloned.1.call-update) | async-done | bytes 11010064 | tf_op jit(solution)/shard_map/all_gather | solution.py:66
  181.3 12.9 %fusion.9 = bf16[1024,1024]{1,0:T(8,128)(2,1)} fusion(bf16[1024,896]{1,0:T(8,128)(2,1)} %get-tuple-element.29, bf16[1024,896]{1,0:T(8,128)(2,1)} %get-tuple-element.36, bf16[1024,896]{1,0:T(8,128)(2,1)S(1)} %get-tuple-element.28, bf16[1024,896]{1,0:T(8,128)(2,1)} %get-tuple-element.37, bf16[1024,5376]{1,0:T(8,128)(2,1)} %all-gather.2.cloned.1.call-done), kind=kOutput, calls=%fused_computation.14 | convolution fusion | flops 7546601472 | bytes 16777216 | tf_op jit(solution)/shard_map/dot_general | solution.py:75
  194.2 5.7 %all-to-all-start.2 = ((bf16[8,128,1024]{2,1,0:T(8,128)(2,1)}), bf16[8,128,1024]{2,1,0:T(8,128)(2,1)S(1)}, u32[]{:S(2)}, u32[]{:S(2)}) async-start(bf16[8,128,1024]{2,1,0:T(8,128)(2,1)} %bitcast.17), calls=%async_computation.3 | async-start | bytes 4194304 | tf_op jit(solution)/shard_map/all_to_all | solution.py:80
  200.0 4.7 %fusion.16 = bf16[1024,896]{1,0:T(8,128)(2,1)S(1)} fusion(bf16[1024,1024]{1,0:T(8,128)(2,1)} %bitcast.13, bf16[1024,5376]{1,0:T(8,128)(2,1)} %all-gather.2.cloned.1.call-done), kind=kOutput, calls=%fused_computation.17 | convolution fusion | flops 1879048192 | bytes 5767168 | tf_op jit(solution)/shard_map/dot_general | solution.py:84
  204.7 4.1 %fusion.20 = bf16[1024,896]{1,0:T(8,128)(2,1)S(1)} fusion(bf16[1024,1024]{1,0:T(8,128)(2,1)S(1)} %bitcast.14, bf16[1024,5376]{1,0:T(8,128)(2,1)} %all-gather.2.cloned.1.call-done), kind=kOutput, calls=%fused_computation.21 | convolution fusion | flops 1879048192 | bytes 5767168 | tf_op jit(solution)/shard_map/dot_general | solution.py:84
  208.8 5.2 %add_convert_fusion.1 = bf16[1024,896]{1,0:T(8,128)(2,1)} fusion(bf16[1024,896]{1,0:T(8,128)(2,1)S(1)} %fusion.20, bf16[1024,1024]{1,0:T(8,128)(2,1)S(1)} %bitcast.15, bf16[1024,5376]{1,0:T(8,128)(2,1)} %all-gather.2.cloned.1.call-done), kind=kOutput, calls=%fused_computation.13 | convolution fusion | flops 1883635712 | bytes 7602176 | tf_op jit(solution)/shard_map/dot_general | solution.py:85
  214.0 5.2 %add_convert_fusion = bf16[1024,896]{1,0:T(8,128)(2,1)} fusion(bf16[1024,896]{1,0:T(8,128)(2,1)S(1)} %fusion.16, bf16[1024,1024]{1,0:T(8,128)(2,1)S(1)} %bitcast.16, bf16[1024,5376]{1,0:T(8,128)(2,1)} %all-gather.2.cloned.1.call-done), kind=kOutput, calls=%fused_computation.12 | convolution fusion | flops 1883635712 | bytes 7602176 | tf_op jit(solution)/shard_map/dot_general | solution.py:85
  219.2 10.4 %all-to-all-done.2 = bf16[8,128,1024]{2,1,0:T(8,128)(2,1)S(1)} async-done(((bf16[8,128,1024]{2,1,0:T(8,128)(2,1)}), bf16[8,128,1024]{2,1,0:T(8,128)(2,1)S(1)}, u32[]{:S(2)}, u32[]{:S(2)}) %all-to-all-start.2) | async-done | bytes 2097184 | tf_op jit(solution)/shard_map/all_to_all | solution.py:80
  229.6 1.1 reduce_sum.12
  (30 shorter events, 6.5 us)
Async XLA Ops:
  7.2 96.9 %reduce-scatter.2.cloned.1.call-start = ((), (), s32[]{:S(2)}) async-start(), calls=%async_computation.4 | async-start | bytes 8257536 | tf_op jit(solution)/shard_map/reduce_scatter | solution.py:29
  8.4 30.9 %copy-start = (bf16[1024,1792]{1,0:T(8,128)(2,1)S(1)}, bf16[1024,1792]{1,0:T(8,128)(2,1)}, u32[]{:S(2)}) copy-start(bf16[1024,1792]{1,0:T(8,128)(2,1)} %param.6) | copy-start | bytes 11010052
  39.4 4.2 %copy-start.2 = (bf16[8,128,1024]{2,1,0:T(8,128)(2,1)}, bf16[8,128,1024]{2,1,0:T(8,128)(2,1)S(1)}, u32[]{:S(2)}) copy-start(bf16[8,128,1024]{2,1,0:T(8,128)(2,1)S(1)} %all_to_all.23) | copy-start | bytes 6291460
  39.4 4.2 %copy-start.1 = (bf16[1024,1792]{1,0:T(8,128)(2,1)S(1)}, bf16[1024,1792]{1,0:T(8,128)(2,1)}, u32[]{:S(2)}) copy-start(bf16[1024,1792]{1,0:T(8,128)(2,1)} %param.5) | copy-start | bytes 11010052
  54.5 0.9 copy-start.7
  55.4 8.1 %collective-permute-start = (bf16[128,1024]{1,0:T(8,128)(2,1)S(1)}, bf16[128,1024]{1,0:T(8,128)(2,1)S(1)}, u32[]{:S(2)}, u32[]{:S(2)}) collective-permute-start(bf16[128,1024]{1,0:T(8,128)(2,1)S(1)} %copy-done.7), channel_id=1, source_target_pairs={{0,1},{1,0},{2,3},{3,2},{4,5},{5,4},{6,7},{7,6},{8,9},{9,8},{10,11... | collective-permute-start | bytes 786440 | tf_op jit(solution)/shard_map/ppermute | solution.py:25
  65.1 5.9 %copy-start.6 = (bf16[128,1792]{1,0:T(8,128)(2,1)S(1)}, bf16[128,1792]{1,0:T(8,128)(2,1)}, u32[]{:S(2)}) copy-start(bf16[128,1792]{1,0:T(8,128)(2,1)} %param.7) | copy-start | bytes 1376260
  65.1 28.5 %all-to-all-start.1 = ((bf16[8,128,1024]{2,1,0:T(8,128)(2,1)}), bf16[8,128,1024]{2,1,0:T(8,128)(2,1)S(1)}, u32[]{:S(2)}, u32[]{:S(2)}) async-start(bf16[8,128,1024]{2,1,0:T(8,128)(2,1)} %tile.5), calls=%async_computation.2 | async-start | bytes 4194304 | tf_op jit(solution)/shard_map/all_to_all | solution.py:23
  71.1 110.3 %all-gather.2.cloned.1.call-start = ((), (), s32[]{:S(2)}) async-start(), calls=%async_computation.5 | async-start | bytes 12386304 | tf_op jit(solution)/shard_map/all_gather | solution.py:66
  93.7 10.4 %copy-start.4 = (bf16[8,128,1024]{2,1,0:T(8,128)(2,1)}, bf16[8,128,1024]{2,1,0:T(8,128)(2,1)S(1)}, u32[]{:S(2)}) copy-start(bf16[8,128,1024]{2,1,0:T(8,128)(2,1)S(1)} %all-to-all-done.1) | copy-start | bytes 6291460
  105.7 13.2 %collective-permute-start.1 = (bf16[128,1792]{1,0:T(8,128)(2,1)S(1)}, bf16[128,1792]{1,0:T(8,128)(2,1)S(1)}, u32[]{:S(2)}, u32[]{:S(2)}) collective-permute-start(bf16[128,1792]{1,0:T(8,128)(2,1)S(1)} %pad_maximum_fusion.1), channel_id=1, source_target_pairs={{0,1},{1,0},{2,3},{3,2},{4,5},{5,4},{6,7},{7,6},{8,9},{9,8},{10,11... | collective-permute-start | bytes 1376264 | tf_op jit(solution)/shard_map/ppermute | solution.py:56
  194.2 35.3 %all-to-all-start.2 = ((bf16[8,128,1024]{2,1,0:T(8,128)(2,1)}), bf16[8,128,1024]{2,1,0:T(8,128)(2,1)S(1)}, u32[]{:S(2)}, u32[]{:S(2)}) async-start(bf16[8,128,1024]{2,1,0:T(8,128)(2,1)} %bitcast.17), calls=%async_computation.3 | async-start | bytes 4194304 | tf_op jit(solution)/shard_map/all_to_all | solution.py:80
  200.0 4.7 %copy-start.3 = (bf16[8,128,1024]{2,1,0:T(8,128)(2,1)S(1)}, bf16[8,128,1024]{2,1,0:T(8,128)(2,1)}, u32[]{:S(2)}) copy-start(bf16[8,128,1024]{2,1,0:T(8,128)(2,1)} %copy-done.2) | copy-start | bytes 6291460
  204.7 4.1 %copy-start.5 = (bf16[8,128,1024]{2,1,0:T(8,128)(2,1)S(1)}, bf16[8,128,1024]{2,1,0:T(8,128)(2,1)}, u32[]{:S(2)}) copy-start(bf16[8,128,1024]{2,1,0:T(8,128)(2,1)} %copy-done.4) | copy-start | bytes 6291460
Sparse Core Ops, SparseCore 0:
  54.6 49.4 reduce-scatter.1
  119.9 61.4 all-gather.1
where the time goes:
time: 238 us
  waiting for transfers between devices  110 us (46%)
  matrix products  41.6 us (17%)
  blocking collectives  30.9 us (13%)
  starting transfers between devices  17.7 us (7%)
  between operations  14.2 us (6%)
  local copies, waits for them, and re-layouts  13.2 us (6%)
  other arithmetic  9.78 us (4%)
    all_gather x1, waiting for transfers between devices, on_device(): lax.all_gather(jnp.concatenate([gate_own, up_own, gate_other, up_other, p...  54.8 us
    all_to_all x1, blocking collectives, gather_col(): return lax.all_to_all(jnp.tile(block, (n_col, 1)), 'col', 0, 0, tiled=True)  30.9 us
    all_to_all x1, waiting for transfers between devices, gather_col(): return lax.all_to_all(jnp.tile(block, (n_col, 1)), 'col', 0, 0, tiled=True)  22.6 us
    dot_general x1, matrix products, on_device(): lax.dot_general(full[:, :2 * width], weights, transposed, preferred_eleme...  12.9 us
    dot_general x2, matrix products, weight_grad(): lax.dot_general(gathered_partner, partner, contract, preferred_element_ty...  10.4 us
    reduce_scatter x1, waiting for transfers between devices, on_device(): lax.psum_scatter(jnp.concatenate([first, second], axis=1).astype(jnp.bflo...  10.4 us
    all_to_all x1, waiting for transfers between devices, on_device(): parts = lax.all_to_all(term, 'col', 0, 0, tiled=True)  10.4 us
    dot_general x2, matrix products, weight_grad(): lax.dot_general(gathered, own, contract, preferred_element_type=jnp.float32)  8.74 us
  transfers between devices with their start and end apart: 6, of which 6 were waited for; matrix products, arithmetic and copies ran while one was open for 13% of the time, Pallas kernels for 0%

commit v1 on v0

--- a/solution.py
+++ b/solution.py
@@ -63,11 +63,21 @@
         grad_gate_other,
         grad_up_other,
     )
-    full = lax.all_gather(
-        jnp.concatenate([gate_own, up_own, gate_other, up_other, partner_gate, partner_up], axis=1),
-        "row",
+    full = jnp.concatenate(
+        lax.all_to_all(
+            jnp.stack(
+                [
+                    jnp.concatenate(
+                        [gate_own, up_own, gate_other, up_other, partner_gate, partner_up], axis=1
+                    )
+                ]
+                * lax.axis_size("row")
+            ),
+            "row",
+            0,
+            0,
+        ),
         axis=0,
-        tiled=True,
     )
     wg_own, wg_other = halves(gate_weight, dep, half)
     wu_own, wu_other = halves(up_weight, dep, half)

time: 238 us -> 305 us (1.28)
  waiting for transfers between devices: 110 us -> 171 us
  starting transfers between devices: 17.7 us -> 22.8 us
    all_to_all x0 -> x1, waiting for transfers between devices: none -> 116 us  [on_device(): lax.all_to_all(jnp.stack([jnp.concatenate([gate_own, up_own, gate_other,...]
    all_gather x1 -> x0, waiting for transfers between devices: 54.8 us -> none  [on_device(): lax.all_gather(jnp.concatenate([gate_own, up_own, gate_other, up_other, p...]
    all_to_all x0 -> x1, starting transfers between devices: none -> 5.2 us  [on_device(): lax.all_to_all(jnp.stack([jnp.concatenate([gate_own, up_own, gate_other,...]
    another operation x0 -> x1, local copies, waits for them, and re-layouts: none -> 4.74 us  [on_device(): jnp.stack([jnp.concatenate([gate_own, up_own, gate_other, up_other, partn...]
    all_to_all x1, waiting for transfers between devices: 10.4 us -> 6.86 us  [on_device(): parts = lax.all_to_all(term, 'col', 0, 0, tiled=True)]
  transfers between devices with their start and end apart: 6 -> 6, of which waited for: 6 -> 6; matrix products, arithmetic and copies ran while one was open for 13% -> 9% of each run, Pallas kernels for 0% -> 0%
where the time goes in v1:
time: 305 us; the launch traced here: 304 us
  waiting for transfers between devices  171 us (56%)
  matrix products  41.6 us (14%)
  blocking collectives  30.9 us (10%)
  starting transfers between devices  22.8 us (7%)
  local copies, waits for them, and re-layouts  15.7 us (5%)
  between operations  14.2 us (5%)
  other arithmetic  8.38 us (3%)
    all_to_all x1, waiting for transfers between devices, on_device(): lax.all_to_all(jnp.stack([jnp.concatenate([gate_own, up_own, gate_other,...  116 us
    all_to_all x1, blocking collectives, gather_col(): return lax.all_to_all(jnp.tile(block, (n_col, 1)), 'col', 0, 0, tiled=True)  30.9 us
    all_to_all x1, waiting for transfers between devices, gather_col(): return lax.all_to_all(jnp.tile(block, (n_col, 1)), 'col', 0, 0, tiled=True)  22.6 us
    dot_general x1, matrix products, on_device(): lax.dot_general(full[:, :2 * width], weights, transposed, preferred_eleme...  12.9 us
    dot_general x2, matrix products, weight_grad(): lax.dot_general(gathered_partner, partner, contract, preferred_element_ty...  10.4 us
    reduce_scatter x1, waiting for transfers between devices, on_device(): lax.psum_scatter(jnp.concatenate([first, second], axis=1).astype(jnp.bflo...  10.4 us
    ppermute x1, waiting for transfers between devices, on_device(): lax.ppermute(payload, 'dep', pair)  9.62 us
    dot_general x2, matrix products, weight_grad(): lax.dot_general(gathered, own, contract, preferred_element_type=jnp.float32)  8.74 us
  transfers between devices with their start and end apart: 6, of which 6 were waited for; matrix products, arithmetic and copies ran while one was open for 9% of the time, Pallas kernels for 0%

profile of v1, /device:TPU:6, one launch (start us, length us, event | category | flops | bytes accessed | tf_op | source)
XLA Modules:
  0.0 304.1 jit_solution(3370863977094159383)
XLA Ops:
  8.4 30.9 %all_to_all.28 = bf16[8,128,1024]{2,1,0:T(8,128)(2,1)S(1)} all-to-all(bf16[8,128,1024]{2,1,0:T(8,128)(2,1)S(1)} %tile.4), channel_id=1, replica_groups=mesh['row'=8,'col'=8,'dep'=2] {'col'}, dimensions={0} | all-to-all | bytes 4194304 | tf_op jit(solution)/shard_map/all_to_all | solution.py:23
  39.4 4.2 %convolution_convert_fusion = bf16[1024,1792]{1,0:T(8,128)(2,1)S(1)} fusion(bf16[1024,1024]{1,0:T(8,128)(2,1)S(1)} %bitcast.12, bf16[1024,1792]{1,0:T(8,128)(2,1)S(1)} %copy-done), kind=kOutput, calls=%fused_computation.10 | convolution fusion | flops 3759931392 | bytes 9437184 | tf_op jit(solution)/shard_map/dot_general | solution.py:28
  43.5 5.4 %convolution_convert_fusion.1 = bf16[1024,1792]{1,0:T(8,128)(2,1)} fusion(bf16[1024,1024]{1,0:T(8,128)(2,1)S(1)} %bitcast.13, bf16[1024,1792]{1,0:T(8,128)(2,1)S(1)} %copy-done.1), kind=kOutput, calls=%fused_computation.11 | convolution fusion | flops 3759931392 | bytes 9437184 | tf_op jit(solution)/shard_map/dot_general | solution.py:27
  48.9 5.6 %pad_maximum_fusion = bf16[1024,3584]{1,0:T(8,128)(2,1)} fusion(bf16[1024,1792]{1,0:T(8,128)(2,1)S(1)} %convolution_convert_fusion, bf16[1024,1792]{1,0:T(8,128)(2,1)} %convolution_convert_fusion.1), kind=kLoop, calls=%fused_computation.2 | loop fusion | flops 14680064 | bytes 14680064 | tf_op jit(solution)/shard_map/concatenate | solution.py:30
  55.4 2.9 collective-permute-start
  58.3 5.2 %collective-permute-done = bf16[128,1024]{1,0:T(8,128)(2,1)S(1)} collective-permute-done((bf16[128,1024]{1,0:T(8,128)(2,1)S(1)}, bf16[128,1024]{1,0:T(8,128)(2,1)S(1)}, u32[]{:S(2)}, u32[]{:S(2)}) %collective-permute-start) | collective-permute-done | bytes 262176 | tf_op jit(solution)/shard_map/ppermute | solution.py:25
  63.5 1.7 tile.5
  65.1 5.9 %all-to-all-start.1 = ((bf16[8,128,1024]{2,1,0:T(8,128)(2,1)}), bf16[8,128,1024]{2,1,0:T(8,128)(2,1)S(1)}, u32[]{:S(2)}, u32[]{:S(2)}) async-start(bf16[8,128,1024]{2,1,0:T(8,128)(2,1)} %tile.5), calls=%async_computation.2 | async-start | bytes 4194304 | tf_op jit(solution)/shard_map/all_to_all | solution.py:23
  71.1 22.6 %all-to-all-done.1 = bf16[8,128,1024]{2,1,0:T(8,128)(2,1)S(1)} async-done(((bf16[8,128,1024]{2,1,0:T(8,128)(2,1)}), bf16[8,128,1024]{2,1,0:T(8,128)(2,1)S(1)}, u32[]{:S(2)}, u32[]{:S(2)}) %all-to-all-start.1) | async-done | bytes 2097184 | tf_op jit(solution)/shard_map/all_to_all | solution.py:23
  93.7 10.4 %reduce-scatter.2.cloned.1.call-done = bf16[128,3584]{1,0:T(8,128)(2,1)} async-done(((bf16[1024,3584]{1,0:T(8,128)(2,1)}), bf16[128,3584]{1,0:T(8,128)(2,1)}) %reduce-scatter.2.cloned.1.call-update) | async-done | bytes 917520 | tf_op jit(solution)/shard_map/reduce_scatter | solution.py:29
  104.1 1.2 fusion.50
  105.7 3.1 %collective-permute-start.1 = (bf16[128,1792]{1,0:T(8,128)(2,1)S(1)}, bf16[128,1792]{1,0:T(8,128)(2,1)S(1)}, u32[]{:S(2)}, u32[]{:S(2)}) collective-permute-start(bf16[128,1792]{1,0:T(8,128)(2,1)S(1)} %pad_maximum_fusion.1), channel_id=1, source_target_pairs={{0,1},{1,0},{2,3},{3,2},{4,5},{5,4},{6,7},{7,6},{8,9},{9,8},{10,11... | collective-permute-start | bytes 1376264 | tf_op jit(solution)/shard_map/ppermute | solution.py:56
  109.2 9.6 %collective-permute-done.1 = bf16[128,1792]{1,0:T(8,128)(2,1)S(1)} collective-permute-done((bf16[128,1792]{1,0:T(8,128)(2,1)S(1)}, bf16[128,1792]{1,0:T(8,128)(2,1)S(1)}, u32[]{:S(2)}, u32[]{:S(2)}) %collective-permute-start.1) | collective-permute-done | bytes 458784 | tf_op jit(solution)/shard_map/ppermute | solution.py:56
  118.9 4.7 %stack.2 = bf16[8,128,5376]{2,1,0:T(8,128)(2,1)} broadcast(bf16[128,5376]{1,0:T(8,128)(2,1)S(1)} %constant_dynamic-update-slice_fusion), dimensions={1,2} | broadcast | bytes 12386304 | tf_op jit(solution)/shard_map/stack | solution.py:68
  123.6 5.2 %all-to-all-start.2 = ((bf16[8,128,5376]{2,1,0:T(8,128)(2,1)}), bf16[8,128,5376]{2,1,0:T(8,128)(2,1)}, u32[]{:S(2)}, u32[]{:S(2)}) async-start(bf16[8,128,5376]{2,1,0:T(8,128)(2,1)} %stack.2), calls=%async_computation.3 | async-start | bytes 22020096 | tf_op jit(solution)/shard_map/all_to_all | solution.py:67
  128.8 5.8 %constant_dynamic-slice_fusion.1 = (bf16[1024,896]{1,0:T(8,128)(2,1)S(1)}, bf16[1024,896]{1,0:T(8,128)(2,1)}, bf16[1024,896]{1,0:T(8,128)(2,1)}, bf16[1024,896]{1,0:T(8,128)(2,1)}) fusion(bf16[1024,1792]{1,0:T(8,128)(2,1)} %param.6, s32[]{:T(128)S(6)} %select_n.5, s32[]{:T(128)S(6)} %select_n.4, bf16[1024,1792]{1,0:T(8,128)(2,1)} %param.5), kind=kLoop, calls=%fused_computation.63 | loop fusion | bytes 14680072 | tf_op jit(solution)/shard_map/dynamic_slice | solution.py:8
  135.6 115.9 %all-to-all-done.2 = bf16[8,128,5376]{2,1,0:T(8,128)(2,1)} async-done(((bf16[8,128,5376]{2,1,0:T(8,128)(2,1)}), bf16[8,128,5376]{2,1,0:T(8,128)(2,1)}, u32[]{:S(2)}, u32[]{:S(2)}) %all-to-all-start.2) | async-done | bytes 11010080 | tf_op jit(solution)/shard_map/all_to_all | solution.py:67
  251.5 12.9 %fusion.9 = bf16[1024,1024]{1,0:T(8,128)(2,1)} fusion(bf16[1024,896]{1,0:T(8,128)(2,1)} %get-tuple-element.29, bf16[1024,896]{1,0:T(8,128)(2,1)} %get-tuple-element.36, bf16[1024,896]{1,0:T(8,128)(2,1)S(1)} %get-tuple-element.28, bf16[1024,896]{1,0:T(8,128)(2,1)} %get-tuple-element.37, bf16[1024,5376]{1,0:T(8,128)(2,1)} %bitcast.2), kind=kOutput, calls=%fused_computation.14 | convolution fusion | flops 7546601472 | bytes 16777216 | tf_op jit(solution)/shard_map/dot_general | solution.py:85
  264.4 5.7 %all-to-all-start.3 = ((bf16[8,128,1024]{2,1,0:T(8,128)(2,1)}), bf16[8,128,1024]{2,1,0:T(8,128)(2,1)S(1)}, u32[]{:S(2)}, u32[]{:S(2)}) async-start(bf16[8,128,1024]{2,1,0:T(8,128)(2,1)} %bitcast.18), calls=%async_computation.4 | async-start | bytes 4194304 | tf_op jit(solution)/shard_map/all_to_all | solution.py:90
  270.1 4.7 %fusion.16 = bf16[1024,896]{1,0:T(8,128)(2,1)S(1)} fusion(bf16[1024,1024]{1,0:T(8,128)(2,1)} %bitcast.14, bf16[1024,5376]{1,0:T(8,128)(2,1)} %bitcast.2), kind=kOutput, calls=%fused_computation.17 | convolution fusion | flops 1879048192 | bytes 5767168 | tf_op jit(solution)/shard_map/dot_general | solution.py:94
  274.8 4.1 %fusion.20 = bf16[1024,896]{1,0:T(8,128)(2,1)S(1)} fusion(bf16[1024,1024]{1,0:T(8,128)(2,1)S(1)} %bitcast.15, bf16[1024,5376]{1,0:T(8,128)(2,1)} %bitcast.2), kind=kOutput, calls=%fused_computation.21 | convolution fusion | flops 1879048192 | bytes 5767168 | tf_op jit(solution)/shard_map/dot_general | solution.py:94
  278.9 5.2 %add_convert_fusion = bf16[1024,896]{1,0:T(8,128)(2,1)} fusion(bf16[1024,896]{1,0:T(8,128)(2,1)S(1)} %fusion.16, bf16[1024,1024]{1,0:T(8,128)(2,1)S(1)} %bitcast.16, bf16[1024,5376]{1,0:T(8,128)(2,1)} %bitcast.2), kind=kOutput, calls=%fused_computation.12 | convolution fusion | flops 1883635712 | bytes 7602176 | tf_op jit(solution)/shard_map/dot_general | solution.py:95
  284.1 5.2 %add_convert_fusion.1 = bf16[1024,896]{1,0:T(8,128)(2,1)} fusion(bf16[1024,896]{1,0:T(8,128)(2,1)S(1)} %fusion.20, bf16[1024,1024]{1,0:T(8,128)(2,1)S(1)} %bitcast.17, bf16[1024,5376]{1,0:T(8,128)(2,1)} %bitcast.2), kind=kOutput, calls=%fused_computation.13 | convolution fusion | flops 1883635712 | bytes 7602176 | tf_op jit(solution)/shard_map/dot_general | solution.py:95
  289.3 6.9 %all-to-all-done.3 = bf16[8,128,1024]{2,1,0:T(8,128)(2,1)S(1)} async-done(((bf16[8,128,1024]{2,1,0:T(8,128)(2,1)}), bf16[8,128,1024]{2,1,0:T(8,128)(2,1)S(1)}, u32[]{:S(2)}, u32[]{:S(2)}) %all-to-all-start.3) | async-done | bytes 2097184 | tf_op jit(solution)/shard_map/all_to_all | solution.py:90
  (30 shorter events, 5.2 us)
Async XLA Ops:
  7.2 96.9 %reduce-scatter.2.cloned.1.call-start = ((), (), s32[]{:S(2)}) async-start(), calls=%async_computation.5 | async-start | bytes 8257536 | tf_op jit(solution)/shard_map/reduce_scatter | solution.py:29
  8.4 30.9 %copy-start = (bf16[1024,1792]{1,0:T(8,128)(2,1)S(1)}, bf16[1024,1792]{1,0:T(8,128)(2,1)}, u32[]{:S(2)}) copy-start(bf16[1024,1792]{1,0:T(8,128)(2,1)} %param.6) | copy-start | bytes 11010052
  39.4 4.2 %copy-start.2 = (bf16[8,128,1024]{2,1,0:T(8,128)(2,1)}, bf16[8,128,1024]{2,1,0:T(8,128)(2,1)S(1)}, u32[]{:S(2)}) copy-start(bf16[8,128,1024]{2,1,0:T(8,128)(2,1)S(1)} %all_to_all.28) | copy-start | bytes 6291460
  39.4 4.2 %copy-start.1 = (bf16[1024,1792]{1,0:T(8,128)(2,1)S(1)}, bf16[1024,1792]{1,0:T(8,128)(2,1)}, u32[]{:S(2)}) copy-start(bf16[1024,1792]{1,0:T(8,128)(2,1)} %param.5) | copy-start | bytes 11010052
  54.5 0.9 copy-start.7
  55.4 8.1 %collective-permute-start = (bf16[128,1024]{1,0:T(8,128)(2,1)S(1)}, bf16[128,1024]{1,0:T(8,128)(2,1)S(1)}, u32[]{:S(2)}, u32[]{:S(2)}) collective-permute-start(bf16[128,1024]{1,0:T(8,128)(2,1)S(1)} %copy-done.7), channel_id=1, source_target_pairs={{0,1},{1,0},{2,3},{3,2},{4,5},{5,4},{6,7},{7,6},{8,9},{9,8},{10,11... | collective-permute-start | bytes 786440 | tf_op jit(solution)/shard_map/ppermute | solution.py:25
  65.1 5.9 %copy-start.6 = (bf16[128,1792]{1,0:T(8,128)(2,1)S(1)}, bf16[128,1792]{1,0:T(8,128)(2,1)}, u32[]{:S(2)}) copy-start(bf16[128,1792]{1,0:T(8,128)(2,1)} %param.7) | copy-start | bytes 1376260
  65.1 28.5 %all-to-all-start.1 = ((bf16[8,128,1024]{2,1,0:T(8,128)(2,1)}), bf16[8,128,1024]{2,1,0:T(8,128)(2,1)S(1)}, u32[]{:S(2)}, u32[]{:S(2)}) async-start(bf16[8,128,1024]{2,1,0:T(8,128)(2,1)} %tile.5), calls=%async_computation.2 | async-start | bytes 4194304 | tf_op jit(solution)/shard_map/all_to_all | solution.py:23
  93.7 10.4 %copy-start.4 = (bf16[8,128,1024]{2,1,0:T(8,128)(2,1)}, bf16[8,128,1024]{2,1,0:T(8,128)(2,1)S(1)}, u32[]{:S(2)}) copy-start(bf16[8,128,1024]{2,1,0:T(8,128)(2,1)S(1)} %all-to-all-done.1) | copy-start | bytes 6291460
  105.7 13.2 %collective-permute-start.1 = (bf16[128,1792]{1,0:T(8,128)(2,1)S(1)}, bf16[128,1792]{1,0:T(8,128)(2,1)S(1)}, u32[]{:S(2)}, u32[]{:S(2)}) collective-permute-start(bf16[128,1792]{1,0:T(8,128)(2,1)S(1)} %pad_maximum_fusion.1), channel_id=1, source_target_pairs={{0,1},{1,0},{2,3},{3,2},{4,5},{5,4},{6,7},{7,6},{8,9},{9,8},{10,11... | collective-permute-start | bytes 1376264 | tf_op jit(solution)/shard_map/ppermute | solution.py:56
  123.6 127.9 %all-to-all-start.2 = ((bf16[8,128,5376]{2,1,0:T(8,128)(2,1)}), bf16[8,128,5376]{2,1,0:T(8,128)(2,1)}, u32[]{:S(2)}, u32[]{:S(2)}) async-start(bf16[8,128,5376]{2,1,0:T(8,128)(2,1)} %stack.2), calls=%async_computation.3 | async-start | bytes 22020096 | tf_op jit(solution)/shard_map/all_to_all | solution.py:67
  264.4 31.8 %all-to-all-start.3 = ((bf16[8,128,1024]{2,1,0:T(8,128)(2,1)}), bf16[8,128,1024]{2,1,0:T(8,128)(2,1)S(1)}, u32[]{:S(2)}, u32[]{:S(2)}) async-start(bf16[8,128,1024]{2,1,0:T(8,128)(2,1)} %bitcast.18), calls=%async_computation.4 | async-start | bytes 4194304 | tf_op jit(solution)/shard_map/all_to_all | solution.py:90
  270.1 4.7 %copy-start.3 = (bf16[8,128,1024]{2,1,0:T(8,128)(2,1)S(1)}, bf16[8,128,1024]{2,1,0:T(8,128)(2,1)}, u32[]{:S(2)}) copy-start(bf16[8,128,1024]{2,1,0:T(8,128)(2,1)} %copy-done.2) | copy-start | bytes 6291460
  274.8 4.1 %copy-start.5 = (bf16[8,128,1024]{2,1,0:T(8,128)(2,1)S(1)}, bf16[8,128,1024]{2,1,0:T(8,128)(2,1)}, u32[]{:S(2)}) copy-start(bf16[8,128,1024]{2,1,0:T(8,128)(2,1)} %copy-done.4) | copy-start | bytes 6291460
Sparse Core Ops, SparseCore 0:
  54.6 49.4 reduce-scatter.1
